TPU v7x, 512 devices: a whole 4x4x16 slice. The times are simulated.
512 devices in a mesh: req: 128 (over z, y, core), wt: 4 (over x).
Axes of the slice: x: 4, y: 4, z: 16, core: 2. Of those that a mesh axis runs over, the one named last changes fastest.
Arguments:
- hidden_in: bfloat16 [32768, 5120], P('req', 'wt'), may hold values from -6 to 6
- queries: bfloat16 [32768, 5120], P('req', 'wt'), as said below
- key_proj: bfloat16 [32768, 5120], P('req', 'wt'), as said below
- values: bfloat16 [32768, 5120], P('req', 'wt'), may hold values from -6 to 6
- query_gain: float32 [5120], P('wt'), may hold values from 0.1 to 1.9
- key_gain: float32 [5120], P('wt'), may hold values from 0.1 to 1.9
- attn_gain: float32 [5120], P('wt'), may hold values from 0.1 to 1.9
- gate_w: bfloat16 [5120, 13824], P('wt', 'req'), may hold values from -0.078125 to 0.078125
- up_w: bfloat16 [5120, 13824], P('wt', 'req'), may hold values from -0.078125 to 0.078125
- lengths: int32 [128], replicated, may hold values from 1 to 256, 4608 in all
- assign: int32 [128], replicated, may hold values from 0 to 127, each once
- page_table: int32 [128, 2], P('req'), may hold values from 0 to 1, each once within a row
Outputs:
- gated: bfloat16 [128, 36, 13824], P(None, 'wt', 'req')
- key_cache: bfloat16 [256, 128, 5120], P('req', None, 'wt')
- value_cache: bfloat16 [256, 128, 5120], P('req', None, 'wt')
Inputs may be any that keep to these rules, and one draw needn't show every extreme that they name: lengths sum to 4608 and at least one request has exactly 256 tokens. `assign`: each device of req serves exactly one request. `page_table`: each row names each of the 2 pages of one device once. `queries`: real-valued entries within -24 to 24. `key_proj`: real-valued entries within -24 to 24.
All inputs are finite; a program needn't handle non-finite values.
Results may differ from a plain program's by a relative error of at most 0.013.
Values may be sent and summed in bfloat16 or wider, within the bound.
No kernel may reach another device: no remote copies, remote signals or barrier semaphores. Data moves between devices by JAX's collectives and lax.ppermute only.
A program may use at most 128 MiB of HBM per device.

v0:
```python
import jax
import jax.numpy as jnp
from jax import lax
from jax.sharding import Mesh, PartitionSpec as P

D = 5120
HD = 128
PAGE = 128
LIVE = 36
EPS = 1e-06
THETA = 500000.0


def rope_tables(row_count, head_width):
    half_width = head_width // 2
    frequency = THETA ** (-(jnp.arange(half_width, dtype=jnp.float32) * 2.0 / head_width))
    angles = jnp.arange(row_count, dtype=jnp.float32)[:, None] * frequency[None, :]
    return (jnp.cos(angles), jnp.sin(angles))


def rotate(heads_in, cosine, sine_table):
    half_width = heads_in.shape[-1] // 2
    leading = heads_in[..., :half_width]
    trailing = heads_in[..., half_width:]
    cos_b = cosine[:, None, :]
    sin_b = sine_table[:, None, :]
    return jnp.concatenate(
        [leading * cos_b - trailing * sin_b, trailing * cos_b + leading * sin_b], axis=-1
    )


def deal_rows(source, owner_start, owner_len, device, owners, live_rows):
    slot_count = source.shape[0]
    feature_count = source.shape[1]
    per_peer = slot_count // owners
    column = jnp.arange(per_peer, dtype=jnp.int32)[None, :]
    target_dev = jnp.arange(owners, dtype=jnp.int32)[:, None]
    my_start = owner_start[device]
    my_length = owner_len[device]
    local_index = (target_dev - my_start) % owners + owners * column
    usable = local_index < my_length
    picked = jnp.where(
        usable[:, :, None],
        source[jnp.minimum(local_index, slot_count - 1)],
        jnp.zeros((), source.dtype),
    )
    arrived = lax.all_to_all(picked, ("ra", "rb"), split_axis=0, concat_axis=0, tiled=True)
    src_start = owner_start[:, None]
    src_length = owner_len[:, None]
    sent_index = (device - src_start) % owners + owners * column
    landing = jnp.where(
        sent_index < src_length, (src_start + sent_index - device) // owners, live_rows
    )
    packed = jnp.zeros((live_rows, feature_count), source.dtype)
    return packed.at[landing.reshape(-1)].set(arrived.reshape(-1, feature_count), mode="drop")


def per_device(
    hidden_in,
    queries,
    key_proj,
    values,
    query_gain,
    key_gain,
    attn_gain,
    gate_w,
    up_w,
    lengths,
    assign,
    page_table,
):
    slot_count = hidden_in.shape[0]
    feature_count = hidden_in.shape[1]
    owners = lax.axis_size(("ra", "rb"))
    device = lax.axis_index("ra") * lax.axis_size("rb") + lax.axis_index("rb")
    head_count = feature_count // HD
    unit_count = gate_w.shape[1]
    owner_req = jnp.zeros((owners,), jnp.int32).at[assign].set(jnp.arange(owners, dtype=jnp.int32))
    starts = jnp.cumsum(lengths) - lengths
    owner_start = starts[owner_req]
    owner_len = lengths[owner_req]
    my_length = owner_len[device]
    query_f = queries.astype(jnp.float32)
    key_f = key_proj.astype(jnp.float32)
    query_sq, key_sq = lax.psum(
        (jnp.sum(query_f * query_f, axis=1), jnp.sum(key_f * key_f, axis=1)), "wt"
    )
    query_n = query_f * lax.rsqrt(query_sq / D + EPS)[:, None] * query_gain
    key_n = key_f * lax.rsqrt(key_sq / D + EPS)[:, None] * key_gain
    cosine, sine_table = rope_tables(slot_count, HD)
    query_r = rotate(query_n.reshape(slot_count, head_count, HD), cosine, sine_table).astype(
        jnp.bfloat16
    )
    key_r = rotate(key_n.reshape(slot_count, head_count, HD), cosine, sine_table).astype(
        jnp.bfloat16
    )
    scores = jnp.einsum(
        "qhd,khd->hqk", query_r, key_r, preferred_element_type=jnp.float32
    ) * HD ** (-0.5)
    position = jnp.arange(slot_count, dtype=jnp.int32)
    allowed = (position[None, :] <= position[:, None]) & (position[None, :] < my_length)
    scores = jnp.where(allowed[None], scores, -jnp.inf)
    row_peak = jnp.max(scores, axis=2, keepdims=True)
    expd = jnp.exp(scores - row_peak)
    probabilities = (expd / jnp.sum(expd, axis=2, keepdims=True)).astype(jnp.bfloat16)
    value_heads = values.reshape(slot_count, head_count, HD)
    attended = jnp.einsum(
        "hqk,khd->qhd", probabilities, value_heads, preferred_element_type=jnp.float32
    )
    attended = attended.astype(jnp.bfloat16).reshape(slot_count, feature_count)
    attended_f = attended.astype(jnp.float32)
    attn_sq = lax.psum(jnp.sum(attended_f * attended_f, axis=1), "wt")
    layer_rows = (
        hidden_in.astype(jnp.float32)
        + attended_f * lax.rsqrt(attn_sq / D + EPS)[:, None] * attn_gain
    ).astype(jnp.bfloat16)
    live_mask = (position < my_length)[:, None]
    page_count = slot_count // PAGE
    zero_value = jnp.zeros((), jnp.bfloat16)
    key_pages = jnp.where(live_mask, key_r.reshape(slot_count, feature_count), zero_value).reshape(
        page_count, PAGE, feature_count
    )
    value_pages = jnp.where(live_mask, values, zero_value).reshape(page_count, PAGE, feature_count)
    placement = page_table[0]
    key_cache = jnp.zeros_like(key_pages).at[placement].set(key_pages)
    value_cache = jnp.zeros_like(value_pages).at[placement].set(value_pages)
    regrouped = deal_rows(layer_rows, owner_start, owner_len, device, owners, LIVE)
    outer = lax.axis_size("ra")
    inner = lax.axis_size("rb")
    piece = lax.all_gather(regrouped, "ra", axis=0, tiled=True)
    weights = lax.all_gather(jnp.stack([gate_w, up_w]), "rb", axis=2, tiled=True)
    stacked = jnp.einsum("tk,skn->tsn", piece, weights, preferred_element_type=jnp.float32)
    stacked = stacked.reshape(outer, LIVE, 2, inner * unit_count)
    summed = lax.psum_scatter(stacked, "wt", scatter_dimension=1, tiled=True)
    gated = (jax.nn.silu(summed[:, :, 0]) * summed[:, :, 1]).astype(jnp.bfloat16)
    rows_here = gated.shape[1]
    gated = gated.reshape(outer, rows_here, inner, unit_count)
    gated = lax.all_to_all(gated, "rb", split_axis=2, concat_axis=2, tiled=True)
    gated = jnp.transpose(gated, (0, 2, 1, 3)).reshape(outer * inner, rows_here, unit_count)
    return (gated, key_cache, value_cache)


def solution(mesh):
    inner = 4
    outer = mesh.shape["req"] // inner
    split = Mesh(mesh.devices.reshape(outer, inner, mesh.shape["wt"]), ("ra", "rb", "wt"))
    req = ("ra", "rb")
    placed = (
        P(req, "wt"),
        P(req, "wt"),
        P(req, "wt"),
        P(req, "wt"),
        P("wt"),
        P("wt"),
        P("wt"),
        P("wt", req),
        P("wt", req),
        P(),
        P(),
        P(req, None),
    )
    return jax.shard_map(
        per_device,
        mesh=split,
        in_specs=placed,
        out_specs=(P(None, "wt", req), P(req, None, "wt"), P(req, None, "wt")),
        check_vma=False,
    )
```

profile of v0, /device:TPU:1, one launch (start us, length us, event | category | flops | bytes accessed | tf_op | source)
XLA Modules:
  0.0 409.6 jit_solution(2444078418245778688)
XLA Ops:
  7.2 0.5 iota_multiply_fusion.1
  7.7 1.3 copy.84
  9.7 9.3 %all-reduce = (f32[256]{0:T(256)S(1)}, f32[256]{0:T(256)S(1)}) all-reduce(f32[256]{0:T(256)S(1)} %fusion.7, f32[256]{0:T(256)S(1)} %fusion.5), channel_id=1, replica_groups=mesh['ra'=32,'rb'=4,'wt'=4] {'wt'}, use_global_device_ids=true, to_apply=%region_5.6 | all-reduce | flops 512 | bytes 4096 | tf_op jit(solution)/shard_map/psum | solution.py:85
  19.0 0.6 add_rsqrt_fusion.1
  19.8 0.9 fusion.40
  20.8 0.4 copy.109
  21.2 1.5 copy.110
  22.7 0.5 fusion.23
  23.2 1.2 compare_select_fusion.4
  24.4 0.5 iota.79
  24.9 1.1 scatter_custom_fusion
  26.1 1.7 gather_fusion.1
  27.8 1.2 dynamic_slice.8
  29.0 0.6 iota_compare_fusion.1
  29.6 0.7 fusion.17
  30.3 0.9 fusion.6
  31.2 0.9 fusion.39
  32.2 1.5 copy.107
  33.7 2.6 copy.108
  36.3 1.1 copy.90
  37.4 0.4 multiply_subtract_fusion
  37.8 0.4 maximum_convert_fusion
  38.1 0.6 copy-done.2
  38.7 0.5 copy-done.1
  39.2 0.4 subtract_convert_fusion
  39.6 0.4 copy-done.7
  40.1 2.7 fusion.42
  42.8 2.1 multiply_reduce_fusion
  45.0 0.4 copy.92
  45.4 6.0 %psum.23 = f32[256]{0:T(256)S(1)} all-reduce(f32[256]{0:T(256)S(1)} %get-tuple-element.33), channel_id=1, replica_groups=mesh['ra'=32,'rb'=4,'wt'=4] {'wt'}, use_global_device_ids=true, to_apply=%region_9.10 | all-reduce | flops 256 | bytes 2048 | tf_op jit(solution)/shard_map/psum | solution.py:112
  51.8 1.2 gather_fusion
  53.0 0.6 dynamic_slice.7
  53.6 0.7 and_select_fusion.1
  54.6 0.3 add_convert_fusion
  54.8 1.2 gather_fusion.2
  56.1 0.2 reshape.448
  56.3 0.3 copy-done.21
  56.7 0.6 add_compare_fusion.2
  57.5 1.5 broadcast_select_fusion
  59.0 23.6 %all-to-all-start = ((bf16[128,2,1280]{2,1,0:T(2,128)(2,1)}), bf16[128,2,1280]{2,1,0:T(2,128)(2,1)S(1)}, u32[]{:S(2)}, u32[]{:S(2)}) async-start(bf16[128,2,1280]{2,1,0:T(2,128)(2,1)} %broadcast_select_fusion), calls=%async_computation | async-start | bytes 1310720 | tf_op jit(solution)/shard_map/all_to_all | solution.py:47
  83.3 35.7 %all-to-all-done = bf16[128,2,1280]{2,1,0:T(2,128)(2,1)S(1)} async-done(((bf16[128,2,1280]{2,1,0:T(2,128)(2,1)}), bf16[128,2,1280]{2,1,0:T(2,128)(2,1)S(1)}, u32[]{:S(2)}, u32[]{:S(2)}) %all-to-all-start) | async-done | bytes 655392 | tf_op jit(solution)/shard_map/all_to_all | solution.py:47
  119.0 0.2 reshape.467
  119.3 2.2 scatter_custom_fusion.1
  121.7 1.2 copy.93
  123.0 140.6 %all-gather.6.cloned.1.call-done = bf16[32,36,1280]{2,1,0:T(8,128)(2,1)} async-done(((bf16[1,36,1280]{2,1,0:T(8,128)(2,1)}), bf16[32,36,1280]{2,1,0:T(8,128)(2,1)}) %all-gather.6.cloned.1.call-update) | async-done | bytes 2949136 | tf_op jit(solution)/shard_map/all_gather | solution.py:130
  263.5 3.7 reshape.493
  267.2 41.0 %all-gather.4.cloned.1.call-done = bf16[2,1280,432]{1,0,2:T(2,128)(2,1)} async-done(((bf16[2,1280,108]{1,0,2:T(2,128)(2,1)}), bf16[2,1280,432]{1,0,2:T(2,128)(2,1)}) %all-gather.4.cloned.1.call-update) | async-done | bytes 2211856 | tf_op jit(solution)/shard_map/all_gather | solution.py:131
  308.2 6.6 %fusion.1 = f32[1152,2,432]{0,2,1:T(8,128)} fusion(bf16[1152,1280,1]{1,0,2:T(8,128)(2,1)S(1)} %reshape.493, bf16[2,1280,432]{1,0,2:T(2,128)(2,1)} %all-gather.4.cloned.1.call-done), kind=kOutput, calls=%fused_computation.11 | convolution fusion | flops 2548039680 | bytes 9142272 | tf_op jit(solution)/shard_map/tk,skn->tsn/dot_general | solution.py:132
  314.8 7.9 %copy.95 = f32[1152,2,432]{2,1,0:T(2,128)} copy(f32[1152,2,432]{0,2,1:T(8,128)} %fusion.1) | data formatting | bytes 7962624 | tf_op jit(solution)/shard_map/tk,skn->tsn/dot_general | solution.py:132
  322.7 7.2 %copy.96 = f32[32,36,2,432]{3,0,2,1:T(8,128)} copy(f32[32,36,2,432]{3,2,1,0:T(2,128)} %bitcast.35) | data formatting | bytes 7962624 | tf_op jit(solution)/shard_map/reshape | solution.py:133
  329.9 1.1 copy-done.8
  331.0 0.5 copy.105
  331.5 0.4 reshape.495
  331.9 0.6 add_compare_fusion.1
  332.7 56.7 %reduce-scatter.2.cloned.1.call-done = f32[32,9,2,432]{3,0,2,1:T(8,128)} async-done(((f32[32,36,2,432]{3,0,2,1:T(8,128)}), f32[32,9,2,432]{3,0,2,1:T(8,128)}) %reduce-scatter.2.cloned.1.call-update) | async-done | bytes 995344 | tf_op jit(solution)/shard_map/reduce_scatter | solution.py:134
  389.4 1.4 fusion.41
  390.7 0.4 squeeze.18
  391.1 0.4 squeeze.19
  391.6 0.9 fusion.16
  392.4 4.0 all-to-all-start.1
  396.5 0.7 scatter_fusion
  397.3 0.7 scatter_fusion.1
  398.1 3.9 all-to-all-done.1
  402.1 0.9 copy.103
  (76 shorter events, 3.2 us)
Async XLA Ops:
  7.2 2.1 copy-start.9
  9.1 10.5 %copy-start.15 = (f32[1280]{0:T(1024)S(1)}, f32[1280]{0:T(1024)}, u32[]{:S(2)}) copy-start(f32[1280]{0:T(1024)} %param.17) | copy-start | bytes 15364
  21.2 4.9 %copy-start = (s32[128]{0:T(128)S(1)}, s32[128]{0:T(128)}, u32[]{:S(2)}) copy-start(s32[128]{0:T(128)} %param.21) | copy-start | bytes 1540
  21.2 9.1 %copy-start.16 = (f32[1280]{0:T(1024)S(1)}, f32[1280]{0:T(1024)}, u32[]{:S(2)}) copy-start(f32[1280]{0:T(1024)} %param.16) | copy-start | bytes 15364
  29.5 0.7 copy-start.19
  33.7 2.6 copy-start.3
  37.4 1.3 copy-start.2
  37.7 1.4 copy-start.1
  39.2 0.8 copy-start.7
  39.2 0.9 copy-start.14
  40.1 2.7 copy-start.10
  44.9 9.4 %copy-start.18 = (s32[2]{0:T(128)S(1)}, s32[2]{0:T(128)}, u32[]{:S(2)}) copy-start(s32[2]{0:T(128)} %iota_multiply_fusion.1) | copy-start | bytes 28
  44.9 9.6 %copy-start.11 = (bf16[256,1280]{1,0:T(8,128)(2,1)S(1)}, bf16[256,1280]{1,0:T(8,128)(2,1)}, u32[]{:S(2)}) copy-start(bf16[256,1280]{1,0:T(8,128)(2,1)} %param.12) | copy-start | bytes 1966084
  45.0 9.6 %copy-start.17 = (f32[1280]{0:T(1024)S(1)}, f32[1280]{0:T(1024)}, u32[]{:S(2)}) copy-start(f32[1280]{0:T(1024)} %param.18) | copy-start | bytes 15364
  56.1 0.6 copy-start.21
  59.0 62.6 %copy-start.12 = (bf16[1280,108]{0,1:T(8,128)(2,1)S(1)}, bf16[1280,108]{0,1:T(8,128)(2,1)}, u32[]{:S(2)}) copy-start(bf16[1280,108]{0,1:T(8,128)(2,1)} %param.20) | copy-start | bytes 829444
  59.0 62.6 %copy-start.13 = (bf16[1280,108]{0,1:T(8,128)(2,1)S(1)}, bf16[1280,108]{0,1:T(8,128)(2,1)}, u32[]{:S(2)}) copy-start(bf16[1280,108]{0,1:T(8,128)(2,1)} %param.19) | copy-start | bytes 829444
  59.0 60.1 %all-to-all-start = ((bf16[128,2,1280]{2,1,0:T(2,128)(2,1)}), bf16[128,2,1280]{2,1,0:T(2,128)(2,1)S(1)}, u32[]{:S(2)}, u32[]{:S(2)}) async-start(bf16[128,2,1280]{2,1,0:T(2,128)(2,1)} %broadcast_select_fusion), calls=%async_computation | async-start | bytes 1310720 | tf_op jit(solution)/shard_map/all_to_all | solution.py:47
  82.6 180.9 %all-gather.6.cloned.1.call-start = ((), (), s32[]{:S(2)}) async-start(), calls=%async_computation.5 | async-start | bytes 3379200 | tf_op jit(solution)/shard_map/all_gather | solution.py:130
  121.5 186.7 %all-gather.4.cloned.1.call-start = ((), (), s32[]{:S(2)}) async-start(), calls=%async_computation.3 | async-start | bytes 2764800 | tf_op jit(solution)/shard_map/all_gather | solution.py:131
  122.9 266.5 %reduce-scatter.2.cloned.1.call-start = ((), (), s32[]{:S(2)}) async-start(), calls=%async_computation.4 | async-start | bytes 5898240 | tf_op jit(solution)/shard_map/reduce_scatter | solution.py:134
  329.9 1.1 copy-start.8
  331.0 1.4 copy-start.4
  331.0 1.5 copy-start.20
  391.5 4.9 %copy-start.22 = (s32[1,2]{1,0:T(1,128)S(1)}, s32[1,2]{1,0:T(1,128)}, u32[]{:S(2)}) copy-start(s32[1,2]{1,0:T(1,128)} %param.23) | copy-start | bytes 28
  392.4 9.6 %all-to-all-start.1 = ((bf16[32,9,4,108]{3,0,1,2:T(8,128)(2,1)}), bf16[32,9,4,108]{3,0,1,2:T(8,128)(2,1)S(1)}, u32[]{:S(2)}, u32[]{:S(2)}) async-start(bf16[32,9,4,108]{3,0,1,2:T(8,128)(2,1)} %fusion.16), calls=%async_computation.2 | async-start | bytes 589824 | tf_op jit(solution)/shard_map/all_to_all | solution.py:138
  397.3 0.8 copy-start.6
  398.1 5.0 %copy-start.5 = (bf16[2,128,1280]{2,1,0:T(8,128)(2,1)}, bf16[2,128,1280]{2,1,0:T(8,128)(2,1)S(1)}, u32[]{:S(2)}) copy-start(bf16[2,128,1280]{2,1,0:T(8,128)(2,1)S(1)} %scatter_fusion.1) | copy-start | bytes 1966084
Sparse Core Ops, SparseCore 0:
  121.7 141.8 all-gather.5
  266.2 41.9 all-gather.3
  330.0 59.3 reduce-scatter.1
where the time goes:
time: 411 us; the launch traced here: 410 us
  waiting for transfers between devices  278 us (68%)
  local copies, waits for them, and re-layouts  50.9 us (12%)
  starting transfers between devices  27.8 us (7%)
  blocking collectives  15.3 us (4%)
  between operations  14.2 us (3%)
  other arithmetic  12.1 us (3%)
  matrix products  11.4 us (3%)
    all_gather x1, waiting for transfers between devices, per_device(): piece = lax.all_gather(regrouped, 'ra', axis=0, tiled=True)  141 us
    reduce_scatter x1, waiting for transfers between devices, per_device(): summed = lax.psum_scatter(stacked, 'wt', scatter_dimension=1, tiled=True)  56.7 us
    all_gather x1, waiting for transfers between devices, per_device(): lax.all_gather(jnp.stack([gate_w, up_w]), 'rb', axis=2, tiled=True)  41 us
    all_to_all x1, waiting for transfers between devices, deal_rows(): lax.all_to_all(picked, ('ra', 'rb'), split_axis=0, concat_axis=0, tiled=T...  35.7 us
    all_to_all x1, starting transfers between devices, deal_rows(): lax.all_to_all(picked, ('ra', 'rb'), split_axis=0, concat_axis=0, tiled=T...  23.6 us
    unnamed x55, local copies, waits for them, and re-layouts  16.3 us
    psum x1, blocking collectives, per_device(): lax.psum((jnp.sum(query_f * query_f, axis=1), jnp.sum(key_f * key_f, axis...  9.29 us
  transfers between devices with their start and end apart: 5, of which 5 were waited for; matrix products, arithmetic and copies ran while one was open for 2% of the time, Pallas kernels for 0%

commit v1 on v0

--- a/solution.py
+++ b/solution.py
@@ -127,7 +127,9 @@
     regrouped = deal_rows(layer_rows, owner_start, owner_len, device, owners, LIVE)
     outer = lax.axis_size("ra")
     inner = lax.axis_size("rb")
-    piece = lax.all_gather(regrouped, "ra", axis=0, tiled=True)
+    piece = jnp.concatenate(
+        lax.all_to_all(jnp.stack([regrouped] * lax.axis_size("ra")), "ra", 0, 0), axis=0
+    )
     weights = lax.all_gather(jnp.stack([gate_w, up_w]), "rb", axis=2, tiled=True)
     stacked = jnp.einsum("tk,skn->tsn", piece, weights, preferred_element_type=jnp.float32)
     stacked = stacked.reshape(outer, LIVE, 2, inner * unit_count)

time: 411 us -> 359 us (0.87)
  waiting for transfers between devices: 278 us -> 235 us
  local copies, waits for them, and re-layouts: 50.9 us -> 34.3 us
  starting transfers between devices: 27.8 us -> 34.4 us
    all_gather x1 -> x0, waiting for transfers between devices: 141 us -> none  [per_device(): piece = lax.all_gather(regrouped, 'ra', axis=0, tiled=True)]
    all_to_all x0 -> x1, waiting for transfers between devices: none -> 98.9 us  [per_device(): lax.all_to_all(jnp.stack([regrouped] * lax.axis_size('ra')), 'ra', 0, 0)]
    dot_general x1 -> x0, local copies, waits for them, and re-layouts: 7.91 us -> none  [per_device(): jnp.einsum('tk,skn->tsn', piece, weights, preferred_element_type=jnp.floa...]
    reshape x1 -> x0, local copies, waits for them, and re-layouts: 7.21 us -> none  [per_device(): stacked = stacked.reshape(outer, LIVE, 2, inner * unit_count)]
    all_to_all x0 -> x1, starting transfers between devices: none -> 6.75 us  [per_device(): lax.all_to_all(jnp.stack([regrouped] * lax.axis_size('ra')), 'ra', 0, 0)]
    reduce_scatter x1, waiting for transfers between devices: 56.7 us -> 52.5 us  [per_device(): summed = lax.psum_scatter(stacked, 'wt', scatter_dimension=1, tiled=True)]
    unnamed x55 -> x50, local copies, waits for them, and re-layouts: 16.3 us -> 12.7 us
where the time goes in v1:
time: 359 us; the launch traced here: 358 us
  waiting for transfers between devices  235 us (65%)
  starting transfers between devices  34.4 us (10%)
  local copies, waits for them, and re-layouts  34.3 us (10%)
  blocking collectives  15.3 us (4%)
  between operations  14.5 us (4%)
  other arithmetic  12.9 us (4%)
  matrix products  11.4 us (3%)
    all_to_all x1, waiting for transfers between devices, per_device(): lax.all_to_all(jnp.stack([regrouped] * lax.axis_size('ra')), 'ra', 0, 0)  98.9 us
    reduce_scatter x1, waiting for transfers between devices, per_device(): summed = lax.psum_scatter(stacked, 'wt', scatter_dimension=1, tiled=True)  52.5 us
    all_gather x1, waiting for transfers between devices, per_device(): lax.all_gather(jnp.stack([gate_w, up_w]), 'rb', axis=2, tiled=True)  44.1 us
    all_to_all x1, waiting for transfers between devices, deal_rows(): lax.all_to_all(picked, ('ra', 'rb'), split_axis=0, concat_axis=0, tiled=T...  35.8 us
    all_to_all x1, starting transfers between devices, deal_rows(): lax.all_to_all(picked, ('ra', 'rb'), split_axis=0, concat_axis=0, tiled=T...  23.5 us
    unnamed x50, local copies, waits for them, and re-layouts  12.7 us
    psum x1, blocking collectives, per_device(): lax.psum((jnp.sum(query_f * query_f, axis=1), jnp.sum(key_f * key_f, axis...  9.29 us
  transfers between devices with their start and end apart: 5, of which 5 were waited for; matrix products, arithmetic and copies ran while one was open for 2% of the time, Pallas kernels for 0%

profile of v1, /device:TPU:1, one launch (start us, length us, event | category | flops | bytes accessed | tf_op | source)
XLA Modules:
  0.0 357.9 jit_solution(16158160334510336585)
XLA Ops:
  7.2 0.5 iota_multiply_fusion.1
  7.7 1.3 copy.74
  9.7 9.3 %all-reduce = (f32[256]{0:T(256)S(1)}, f32[256]{0:T(256)S(1)}) all-reduce(f32[256]{0:T(256)S(1)} %fusion.9, f32[256]{0:T(256)S(1)} %fusion.7), channel_id=1, replica_groups=mesh['ra'=32,'rb'=4,'wt'=4] {'wt'}, use_global_device_ids=true, to_apply=%region_5.6 | all-reduce | flops 512 | bytes 4096 | tf_op jit(solution)/shard_map/psum | solution.py:85
  19.0 0.6 add_rsqrt_fusion.1
  19.8 0.9 fusion.43
  20.8 0.4 copy.98
  21.2 1.5 copy.99
  22.7 0.5 fusion.26
  23.2 1.2 compare_select_fusion.4
  24.4 0.5 iota.79
  24.9 1.1 scatter_custom_fusion
  26.0 1.8 gather_fusion.1
  27.8 1.3 dynamic_slice.8
  29.1 0.7 iota_compare_fusion.1
  29.9 0.7 fusion.20
  30.6 0.9 fusion.8
  31.5 0.9 fusion.42
  32.5 1.5 copy.96
  33.9 2.6 copy.97
  36.6 1.1 copy.80
  37.7 0.4 multiply_subtract_fusion
  38.0 0.4 maximum_convert_fusion
  38.4 0.6 copy-done.2
  39.0 0.5 copy-done.1
  39.5 0.4 subtract_convert_fusion
  39.9 0.4 copy-done.7
  40.3 2.7 fusion.45
  43.1 2.1 multiply_reduce_fusion
  45.2 0.4 copy.82
  45.6 6.0 %psum.23 = f32[256]{0:T(256)S(1)} all-reduce(f32[256]{0:T(256)S(1)} %get-tuple-element.33), channel_id=1, replica_groups=mesh['ra'=32,'rb'=4,'wt'=4] {'wt'}, use_global_device_ids=true, to_apply=%region_9.10 | all-reduce | flops 256 | bytes 2048 | tf_op jit(solution)/shard_map/psum | solution.py:112
  52.1 1.2 gather_fusion
  53.3 0.6 dynamic_slice.7
  53.9 0.7 and_select_fusion.1
  54.8 0.3 add_convert_fusion
  55.1 1.2 gather_fusion.2
  56.4 0.2 reshape.450
  56.6 0.4 copy-done.19
  57.0 0.8 add_compare_fusion.2
  57.9 1.5 broadcast_select_fusion
  59.4 23.5 %all-to-all-start = ((bf16[128,2,1280]{2,1,0:T(2,128)(2,1)}), bf16[128,2,1280]{2,1,0:T(2,128)(2,1)S(1)}, u32[]{:S(2)}, u32[]{:S(2)}) async-start(bf16[128,2,1280]{2,1,0:T(2,128)(2,1)} %broadcast_select_fusion), calls=%async_computation | async-start | bytes 1310720 | tf_op jit(solution)/shard_map/all_to_all | solution.py:47
  83.6 35.8 %all-to-all-done = bf16[128,2,1280]{2,1,0:T(2,128)(2,1)S(1)} async-done(((bf16[128,2,1280]{2,1,0:T(2,128)(2,1)}), bf16[128,2,1280]{2,1,0:T(2,128)(2,1)S(1)}, u32[]{:S(2)}, u32[]{:S(2)}) %all-to-all-start) | async-done | bytes 655392 | tf_op jit(solution)/shard_map/all_to_all | solution.py:47
  119.6 1.6 scatter_custom_fusion.1
  121.2 1.9 stack.8
  123.1 6.8 %all-to-all-start.1 = ((bf16[32,36,1280]{2,1,0:T(8,128)(2,1)}), bf16[32,36,1280]{2,1,0:T(8,128)(2,1)S(1)}, u32[]{:S(2)}, u32[]{:S(2)}) async-start(bf16[32,36,1280]{2,1,0:T(8,128)(2,1)} %stack.8), calls=%async_computation.1 | async-start | bytes 6553600 | tf_op jit(solution)/shard_map/all_to_all | solution.py:131
  129.9 1.1 pad_maximum_fusion
  131.1 1.2 copy.83
  132.4 44.1 %all-gather.2.cloned.1.call-done = bf16[2,1280,432]{1,0,2:T(2,128)(2,1)} async-done(((bf16[2,1280,108]{1,0,2:T(2,128)(2,1)}), bf16[2,1280,432]{1,0,2:T(2,128)(2,1)}) %all-gather.2.cloned.1.call-update) | async-done | bytes 2211856 | tf_op jit(solution)/shard_map/all_gather | solution.py:133
  176.4 98.9 %all-to-all-done.1 = bf16[32,36,1280]{2,1,0:T(8,128)(2,1)S(1)} async-done(((bf16[32,36,1280]{2,1,0:T(8,128)(2,1)}), bf16[32,36,1280]{2,1,0:T(8,128)(2,1)S(1)}, u32[]{:S(2)}, u32[]{:S(2)}) %all-to-all-start.1) | async-done | bytes 2949152 | tf_op jit(solution)/shard_map/all_to_all | solution.py:131
  275.3 6.5 %fusion.1 = f32[32,36,2,432]{3,0,2,1:T(8,128)} fusion(bf16[32,36,1280,1]{2,1,0,3:T(8,128)(2,1)S(1)} %bitcast.38, bf16[2,1280,432]{1,0,2:T(2,128)(2,1)} %all-gather.2.cloned.1.call-done), kind=kOutput, calls=%fused_computation.8 | convolution fusion | flops 2548039680 | bytes 9142272 | tf_op jit(solution)/shard_map/tk,skn->tsn/dot_general | solution.py:134
  281.8 1.1 copy-done.8
  282.9 0.5 copy.94
  283.4 0.4 reshape.495
  283.8 0.7 add_compare_fusion.1
  284.7 52.5 %reduce-scatter.2.cloned.1.call-done = f32[32,9,2,432]{3,0,2,1:T(8,128)} async-done(((f32[32,36,2,432]{3,0,2,1:T(8,128)}), f32[32,9,2,432]{3,0,2,1:T(8,128)}) %reduce-scatter.2.cloned.1.call-update) | async-done | bytes 995344 | tf_op jit(solution)/shard_map/reduce_scatter | solution.py:136
  337.2 1.4 fusion.44
  338.6 0.4 squeeze.18
  339.0 0.4 squeeze.19
  339.4 0.3 fusion.19
  339.7 0.8 copy.86
  340.5 4.0 %all-to-all-start.2 = ((bf16[32,9,4,108]{3,0,1,2:T(8,128)(2,1)}), bf16[32,9,4,108]{3,0,1,2:T(8,128)(2,1)S(1)}, u32[]{:S(2)}, u32[]{:S(2)}) async-start(bf16[32,9,4,108]{3,0,1,2:T(8,128)(2,1)} %copy.86), calls=%async_computation.3 | async-start | bytes 589824 | tf_op jit(solution)/shard_map/all_to_all | solution.py:140
  344.6 0.7 scatter_fusion
  345.4 0.7 scatter_fusion.1
  346.2 3.9 %all-to-all-done.2 = bf16[32,9,4,108]{3,0,1,2:T(8,128)(2,1)S(1)} async-done(((bf16[32,9,4,108]{3,0,1,2:T(8,128)(2,1)}), bf16[32,9,4,108]{3,0,1,2:T(8,128)(2,1)S(1)}, u32[]{:S(2)}, u32[]{:S(2)}) %all-to-all-start.2) | async-done | bytes 248864 | tf_op jit(solution)/shard_map/all_to_all | solution.py:140
  350.2 0.9 copy.90
  (70 shorter events, 3.3 us)
Async XLA Ops:
  7.2 2.1 copy-start.9
  9.0 10.5 %copy-start.13 = (f32[1280]{0:T(1024)S(1)}, f32[1280]{0:T(1024)}, u32[]{:S(2)}) copy-start(f32[1280]{0:T(1024)} %param.17) | copy-start | bytes 15364
  21.2 4.9 %copy-start = (s32[128]{0:T(128)S(1)}, s32[128]{0:T(128)}, u32[]{:S(2)}) copy-start(s32[128]{0:T(128)} %param.21) | copy-start | bytes 1540
  21.2 9.4 %copy-start.14 = (f32[1280]{0:T(1024)S(1)}, f32[1280]{0:T(1024)}, u32[]{:S(2)}) copy-start(f32[1280]{0:T(1024)} %param.16) | copy-start | bytes 15364
  29.8 0.7 copy-start.17
  33.9 2.6 copy-start.3
  37.7 1.3 copy-start.2
  38.0 1.4 copy-start.1
  39.5 0.8 copy-start.7
  39.5 0.9 copy-start.12
  40.3 2.7 copy-start.10
  45.2 9.4 %copy-start.16 = (s32[2]{0:T(128)S(1)}, s32[2]{0:T(128)}, u32[]{:S(2)}) copy-start(s32[2]{0:T(128)} %iota_multiply_fusion.1) | copy-start | bytes 28
  45.2 9.6 %copy-start.11 = (bf16[256,1280]{1,0:T(8,128)(2,1)S(1)}, bf16[256,1280]{1,0:T(8,128)(2,1)}, u32[]{:S(2)}) copy-start(bf16[256,1280]{1,0:T(8,128)(2,1)} %param.12) | copy-start | bytes 1966084
  45.2 9.6 %copy-start.15 = (f32[1280]{0:T(1024)S(1)}, f32[1280]{0:T(1024)}, u32[]{:S(2)}) copy-start(f32[1280]{0:T(1024)} %param.18) | copy-start | bytes 15364
  56.3 0.7 copy-start.19
  59.4 59.9 %all-to-all-start = ((bf16[128,2,1280]{2,1,0:T(2,128)(2,1)}), bf16[128,2,1280]{2,1,0:T(2,128)(2,1)S(1)}, u32[]{:S(2)}, u32[]{:S(2)}) async-start(bf16[128,2,1280]{2,1,0:T(2,128)(2,1)} %broadcast_select_fusion), calls=%async_computation | async-start | bytes 1310720 | tf_op jit(solution)/shard_map/all_to_all | solution.py:47
  123.1 152.2 %all-to-all-start.1 = ((bf16[32,36,1280]{2,1,0:T(8,128)(2,1)}), bf16[32,36,1280]{2,1,0:T(8,128)(2,1)S(1)}, u32[]{:S(2)}, u32[]{:S(2)}) async-start(bf16[32,36,1280]{2,1,0:T(8,128)(2,1)} %stack.8), calls=%async_computation.1 | async-start | bytes 6553600 | tf_op jit(solution)/shard_map/all_to_all | solution.py:131
  129.9 46.5 %all-gather.2.cloned.1.call-start = ((), (), s32[]{:S(2)}) async-start(), calls=%async_computation.4 | async-start | bytes 2764800 | tf_op jit(solution)/shard_map/all_gather | solution.py:133
  132.3 204.9 %reduce-scatter.2.cloned.1.call-start = ((), (), s32[]{:S(2)}) async-start(), calls=%async_computation.5 | async-start | bytes 5898240 | tf_op jit(solution)/shard_map/reduce_scatter | solution.py:136
  281.8 1.1 copy-start.8
  282.9 1.6 copy-start.4
  282.9 1.6 copy-start.18
  339.4 5.1 %copy-start.20 = (s32[1,2]{1,0:T(1,128)S(1)}, s32[1,2]{1,0:T(1,128)}, u32[]{:S(2)}) copy-start(s32[1,2]{1,0:T(1,128)} %param.23) | copy-start | bytes 28
  340.5 9.6 %all-to-all-start.2 = ((bf16[32,9,4,108]{3,0,1,2:T(8,128)(2,1)}), bf16[32,9,4,108]{3,0,1,2:T(8,128)(2,1)S(1)}, u32[]{:S(2)}, u32[]{:S(2)}) async-start(bf16[32,9,4,108]{3,0,1,2:T(8,128)(2,1)} %copy.86), calls=%async_computation.3 | async-start | bytes 589824 | tf_op jit(solution)/shard_map/all_to_all | solution.py:140
  345.3 0.8 copy-start.6
  346.2 5.0 %copy-start.5 = (bf16[2,128,1280]{2,1,0:T(8,128)(2,1)}, bf16[2,128,1280]{2,1,0:T(8,128)(2,1)S(1)}, u32[]{:S(2)}) copy-start(bf16[2,128,1280]{2,1,0:T(8,128)(2,1)S(1)} %scatter_fusion.1) | copy-start | bytes 1966084
Sparse Core Ops, SparseCore 0:
  133.4 42.9 all-gather.1
  282.0 55.2 reduce-scatter.1
